TPU v7x, 128 devices: a whole 4x4x4 slice. The times are simulated.
128 devices in a mesh: req: 4 (over z), seq: 32 (over x, y, core).
Axes of the slice: x: 4, y: 4, z: 4, core: 2. Of those that a mesh axis runs over, the one named last changes fastest.
Arguments:
- short_tokens: bfloat16 [256, 4, 1024], P(('req', 'seq')), may hold values from -6 to 6
- long_tokens: bfloat16 [8, 4, 1024], P('req'), may hold values from -6 to 6
- short_keys: bfloat16 [256, 1024, 1024], P(('req', 'seq'))
- short_values: bfloat16 [256, 1024, 1024], P(('req', 'seq')), may hold values from -6 to 6
- long_keys: bfloat16 [8, 8192, 1024], P('req', 'seq')
- long_values: bfloat16 [8, 8192, 1024], P('req', 'seq'), may hold values from -6 to 6
- short_lengths: int32 [256], P(('req', 'seq')), may hold values from 512 to 1024
- long_lengths: int32 [8], P('req'), may hold values from 4096 to 8192
- attn_gain: float32 [1024], replicated, may hold values from 0.5 to 1.5
- ffn_gain: float32 [1024], replicated, may hold values from 0.5 to 1.5
- w_query: bfloat16 [1024, 1024], P(None, 'req'), may hold values from -0.1875 to 0.1875
- w_key: bfloat16 [1024, 1024], P(None, 'req'), may hold values from -0.1875 to 0.1875
- w_value: bfloat16 [1024, 1024], P(None, 'req'), may hold values from -0.1875 to 0.1875
- w_out: bfloat16 [1024, 1024], P('req'), may hold values from -0.1875 to 0.1875
- w_up: bfloat16 [1024, 4096], P(None, 'req'), may hold values from -0.1875 to 0.1875
- w_down: bfloat16 [4096, 1024], P('req'), may hold values from -0.09375 to 0.09375
Outputs:
- short_hidden: bfloat16 [256, 4, 1024], P(('req', 'seq'))
- long_hidden: bfloat16 [8, 4, 1024], P('req')
- short_new_keys: bfloat16 [256, 4, 1024], P(('req', 'seq'))
- short_new_values: bfloat16 [256, 4, 1024], P(('req', 'seq'))
- long_new_keys: bfloat16 [8, 4, 1024], P('req')
- long_new_values: bfloat16 [8, 4, 1024], P('req')
All inputs are finite; a program needn't handle non-finite values.
Results may differ from a plain program's by a relative error of at most 0.011.
Values may be sent and summed in bfloat16 or wider, within the bound.
No kernel may reach another device: no remote copies, remote signals or barrier semaphores. Data moves between devices by JAX's collectives and lax.ppermute only.
A program may use at most 128 MiB of HBM per device.

v0:
```python
import jax
import jax.numpy as jnp
from jax import lax
from jax.sharding import PartitionSpec as P

H = 16
HD = 64
masked_score = -1e30


def layer_norm(rows, gain):
    mean = jnp.mean(rows, axis=-1, keepdims=True)
    centred = rows - mean
    spread = jnp.mean(centred * centred, axis=-1, keepdims=True)
    return centred * lax.rsqrt(spread + 1e-05) * gain


def partial_block(query, keys, values, valid):
    scores = jnp.einsum("rthd,rphd->rthp", query, keys, preferred_element_type=jnp.float32) * 0.125
    scores = jnp.where(valid, scores, masked_score)
    peak = jnp.max(scores, axis=-1)
    weights = jnp.where(valid, jnp.exp(scores - peak[..., None]), 0.0)
    total = jnp.sum(weights, axis=-1)
    output = jnp.einsum(
        "rthp,rphd->rthd", weights.astype(jnp.bfloat16), values, preferred_element_type=jnp.float32
    )
    return (peak, total, output)


def cache_block(query, keys, values, valid):
    reqs, steps = (query.shape[0], query.shape[1])
    eye = jnp.eye(H, dtype=query.dtype)
    spread = (query[:, :, :, None, :] * eye[None, None, :, :, None]).reshape(
        reqs, steps * H, H * HD
    )
    scores = jnp.einsum("rnc,rpc->rnp", spread, keys, preferred_element_type=jnp.float32) * 0.125
    scores = jnp.where(valid, scores, masked_score)
    peak = jnp.max(scores, axis=-1)
    weights = jnp.where(valid, jnp.exp(scores - peak[..., None]), 0.0)
    total = jnp.sum(weights, axis=-1)
    full = jnp.einsum(
        "rnp,rpc->rnc", weights.astype(jnp.bfloat16), values, preferred_element_type=jnp.float32
    ).reshape(reqs, steps, H, H, HD)
    output = jnp.sum(full * eye.astype(jnp.float32)[None, None, :, :, None], axis=3)
    return (peak.reshape(reqs, steps, H), total.reshape(reqs, steps, H), output)


def join(first, second):
    peak = jnp.maximum(first[0], second[0])
    scale_one = jnp.exp(first[0] - peak)
    scale_two = jnp.exp(second[0] - peak)
    total = first[1] * scale_one + second[1] * scale_two
    output = first[2] * scale_one[..., None] + second[2] * scale_two[..., None]
    return (peak, total, output)


def merge_long(partial_value):
    peak, total, output = partial_value
    packed = jnp.concatenate([output, peak[..., None], total[..., None]], -1)
    size = lax.axis_size("seq")
    me = lax.axis_index("seq")
    width = output.shape[-1]
    distance = 1
    while distance < size:
        pairs = [(i, i ^ distance) for i in range(size)]
        other = lax.ppermute(packed, "seq", pairs)
        lower = me & distance == 0
        first = jnp.where(lower, packed, other)
        second = jnp.where(lower, other, packed)
        top = jnp.maximum(first[..., width], second[..., width])
        scale_one = jnp.exp(first[..., width] - top)[..., None]
        scale_two = jnp.exp(second[..., width] - top)[..., None]
        merged = first[..., :width] * scale_one + second[..., :width] * scale_two
        summed = first[..., width + 1 :] * scale_one + second[..., width + 1 :] * scale_two
        packed = jnp.concatenate([merged, top[..., None], summed], -1)
        distance *= 2
    return (packed[..., width], packed[..., width + 1], packed[..., :width])


def shards(
    short_tokens,
    long_tokens,
    short_keys,
    short_values,
    long_keys,
    long_values,
    short_lengths,
    long_lengths,
    attn_gain,
    ffn_gain,
    w_query,
    w_key,
    w_value,
    w_out,
    w_up,
    w_down,
):
    short_count = short_tokens.shape[0]
    long_count = long_tokens.shape[0]
    steps = short_tokens.shape[1]
    width = short_tokens.shape[2]
    req_count = short_count + long_count
    rows_count = req_count * steps
    groups = lax.axis_size("req")
    block = long_keys.shape[1]
    anchor = lax.axis_index("seq") * block
    short_valid = (jnp.arange(short_keys.shape[1])[None, :] < short_lengths[:, None])[:, None, :]
    long_valid = ((anchor + jnp.arange(block))[None, :] < long_lengths[:, None])[:, None, :]
    w_out_full = lax.all_gather(w_out, "req", axis=0, tiled=True)
    stacked = jnp.concatenate([w_query, w_key, w_value], 1)
    local = w_query.shape[1]
    fresh_ids = jnp.arange(steps)
    fresh_valid = (fresh_ids[None, :] <= fresh_ids[:, None])[None, :, None, :]
    rows = (
        jnp.concatenate([short_tokens, long_tokens], 0)
        .reshape(rows_count, width)
        .astype(jnp.float32)
    )
    normed = layer_norm(rows, attn_gain).astype(jnp.bfloat16)
    project_spread = jnp.dot(
        lax.all_gather(normed, "req", axis=0, tiled=True),
        stacked,
        preferred_element_type=jnp.float32,
    ).astype(jnp.bfloat16)
    moved = lax.all_to_all(project_spread, "req", split_axis=0, concat_axis=1, tiled=True)
    moved = moved.reshape(rows_count, groups, 3, local)
    query = moved[:, :, 0].reshape(req_count, steps, H, HD)
    key_now = moved[:, :, 1].reshape(req_count, steps, width)
    value_now = moved[:, :, 2].reshape(req_count, steps, width)
    fresh_k = key_now.reshape(req_count, steps, H, HD)
    fresh_v = value_now.reshape(req_count, steps, H, HD)
    fresh = partial_block(query, fresh_k, fresh_v, fresh_valid)
    short_part = cache_block(query[:short_count], short_keys, short_values, short_valid)
    long_part = merge_long(cache_block(query[short_count:], long_keys, long_values, long_valid))
    cache_part = jax.tree.map(
        lambda first, second: jnp.concatenate([first, second], 0), short_part, long_part
    )
    peak, total, output = join(cache_part, fresh)
    attended = output / total[..., None]
    attended = attended.reshape(rows_count, width).astype(jnp.bfloat16)
    mixed = rows + jnp.dot(attended, w_out_full, preferred_element_type=jnp.float32)
    normed_ffn = layer_norm(mixed, ffn_gain).astype(jnp.bfloat16)
    hidden = jax.nn.gelu(
        jnp.dot(
            lax.all_gather(normed_ffn, "req", axis=0, tiled=True),
            w_up,
            preferred_element_type=jnp.float32,
        ),
        approximate=False,
    ).astype(jnp.bfloat16)
    result = mixed + lax.psum_scatter(
        jnp.dot(hidden, w_down, preferred_element_type=jnp.float32),
        "req",
        scatter_dimension=0,
        tiled=True,
    )
    states = result.astype(jnp.bfloat16).reshape(req_count, steps, width)
    return (
        states[:short_count],
        states[short_count:],
        key_now[:short_count],
        value_now[:short_count],
        key_now[short_count:],
        value_now[short_count:],
    )


def solution(mesh):
    in_specs = (
        P(("req", "seq"), None, None),
        P("req", None, None),
        P(("req", "seq"), None, None),
        P(("req", "seq"), None, None),
        P("req", "seq", None),
        P("req", "seq", None),
        P(("req", "seq")),
        P("req"),
        P(),
        P(),
        P(None, "req"),
        P(None, "req"),
        P(None, "req"),
        P("req", None),
        P(None, "req"),
        P("req", None),
    )
    out_specs = (
        P(("req", "seq"), None, None),
        P("req", None, None),
        P(("req", "seq"), None, None),
        P(("req", "seq"), None, None),
        P("req", None, None),
        P("req", None, None),
    )
    return jax.shard_map(shards, mesh=mesh, in_specs=in_specs, out_specs=out_specs, check_vma=False)
```

profile of v0, /device:TPU:0, one launch (start us, length us, event | category | flops | bytes accessed | tf_op | source)
XLA Modules:
  0.0 143.6 jit_solution(11437856707310155101)
XLA Ops:
  10.8 13.3 %all_gather.9 = bf16[64,1024]{1,0:T(8,128)(2,1)S(1)} all-gather(bf16[16,1024]{1,0:T(8,128)(2,1)S(1)} %multiply_convert_fusion.1), channel_id=1, replica_groups=mesh['req'=4,'seq'=32] {'req'}, dimensions={0}, use_global_device_ids=true | all-gather | bytes 163840 | tf_op jit(solution)/shard_map/all_gather | solution.py:121
  24.1 2.4 %fusion.7 = bf16[64,768]{1,0:T(8,128)(2,1)} fusion(bf16[64,1024]{1,0:T(8,128)(2,1)S(1)} %all_gather.9, bf16[1024,256]{1,0:T(8,128)(2,1)} %param.28, bf16[1024,256]{1,0:T(8,128)(2,1)} %param.27, bf16[1024,256]{1,0:T(8,128)(2,1)} %param.26), kind=kOutput, calls=%fused_computation.8 | convolution fusion | flops 105431040 | bytes 1802240 | tf_op jit(solution)/shard_map/dot_general | solution.py:120
  26.5 4.3 %all-to-all-start = ((bf16[4,16,768]{2,1,0:T(8,128)(2,1)}), bf16[4,16,768]{2,1,0:T(8,128)(2,1)S(1)}, u32[]{:S(2)}, u32[]{:S(2)}) async-start(bf16[4,16,768]{2,1,0:T(8,128)(2,1)} %bitcast), calls=%async_computation | async-start | bytes 196608 | tf_op jit(solution)/shard_map/all_to_all | solution.py:125
  32.6 4.0 %all-to-all-done = bf16[4,16,768]{2,1,0:T(8,128)(2,1)S(1)} async-done(((bf16[4,16,768]{2,1,0:T(8,128)(2,1)}), bf16[4,16,768]{2,1,0:T(8,128)(2,1)S(1)}, u32[]{:S(2)}, u32[]{:S(2)}) %all-to-all-start) | async-done | bytes 98336 | tf_op jit(solution)/shard_map/all_to_all | solution.py:125
  38.8 1.8 %fusion.147 = (f32[2,64]{1,0:T(2,128)S(1)}, f32[2,64,256]{2,1,0:T(8,128)S(1)}) fusion(bf16[2,256,1024]{2,1,0:T(8,128)(2,1)} %param.20, bf16[2,64,1024]{2,1,0:T(8,128)(2,1)S(1)} %mul.317, bf16[64,1024]{1,0:T(8,128)(2,1)S(1)} %mul.307, pred[2,256]{1,0:T(4,128)(4,1)S(1)} %broadcast_compare_fusion), kind=kOutput, calls=%fused_computation.229 | convolution fusion | flops 67338112 | bytes 1573888 | tf_op jit(solution)/shard_map/rnc,rpc->rnp/dot_general | solution.py:36
  40.8 1.6 %fusion.74 = f32[2,64,1024]{2,1,0:T(8,128)S(1)} fusion(bf16[2,256,1024]{2,1,0:T(8,128)(2,1)} %param.21, f32[2,64,256]{2,1,0:T(8,128)S(1)} %get-tuple-element.55, f32[2,64]{1,0:T(2,128)S(1)} %get-tuple-element.54, pred[2,256]{1,0:T(4,128)(4,1)S(1)} %broadcast_compare_fusion), kind=kOutput, calls=%fused_computation.113 | convolution fusion | flops 67207168 | bytes 1704960 | tf_op jit(solution)/shard_map/rnp,rpc->rnc/dot_general | solution.py:41
  42.4 1.3 reshape.257
  44.3 4.1 %fusion.148 = (f32[2,64]{1,0:T(2,128)S(1)}, f32[2,64,1024]{2,1,0:T(8,128)S(1)}) fusion(bf16[2,1024,1024]{2,1,0:T(8,128)(2,1)} %param.18, bf16[2,64,1024]{2,1,0:T(8,128)(2,1)S(1)} %mul.305, bf16[64,1024]{1,0:T(8,128)(2,1)S(1)} %mul.307, pred[2,1024]{1,0:T(4,128)(4,1)S(1)} %iota_compare_fusion.1), kind=kOutput, calls=%fused_computation.230 | convolution fusion | flops 268959616 | bytes 5114368 | tf_op jit(solution)/shard_map/rnc,rpc->rnp/dot_general | solution.py:36
  49.3 1.2 reshape.256
  50.5 2.1 %multiply_reduce_fusion.1 = (f32[2,4,16,64]{3,2,1,0:T(8,128)S(1)}, f32[2,4,16,64]{3,2,1,0:T(8,128)S(1)}) fusion(f32[2,4,16,16,64]{4,3,2,1,0:T(8,128)} %reshape.256, f32[16,16]{1,0:T(8,128)S(1)} %fusion.97, f32[2,4,16,16,64]{4,3,2,1,0:T(8,128)} %reshape.257), kind=kLoop, calls=%fused_computation.13 | loop fusion | flops 507904 | bytes 1115136 | tf_op jit(solution)/shard_map/reduce_sum | solution.py:44
  55.2 1.1 broadcast_select_fusion.1
  56.5 1.7 %collective-permute-start.1 = (f32[2,4,16,66]{2,1,3,0:T(4,128)S(1)}, f32[2,4,16,66]{2,1,3,0:T(4,128)S(1)}, u32[]{:S(2)}, u32[]{:S(2)}) collective-permute-start(f32[2,4,16,66]{2,1,3,0:T(4,128)S(1)} %pad_maximum_fusion.1), channel_id=1, source_target_pairs={{0,2},{1,3},{2,0},{3,1},{4,6},{5,7},{6,4},{7,5},{8,10},{9,11},{10,... | collective-permute-start | bytes 101384 | tf_op jit(solution)/shard_map/ppermute | solution.py:66
  58.3 7.2 %collective-permute-done.1 = f32[2,4,16,66]{2,1,3,0:T(4,128)S(1)} collective-permute-done((f32[2,4,16,66]{2,1,3,0:T(4,128)S(1)}, f32[2,4,16,66]{2,1,3,0:T(4,128)S(1)}, u32[]{:S(2)}, u32[]{:S(2)}) %collective-permute-start.1) | collective-permute-done | bytes 33824 | tf_op jit(solution)/shard_map/ppermute | solution.py:66
  65.8 3.3 %collective-permute-start.2 = (f32[2,4,16,66]{2,1,3,0:T(4,128)S(1)}, f32[2,4,16,66]{2,1,3,0:T(4,128)}, u32[]{:S(2)}, u32[]{:S(2)}) collective-permute-start(f32[2,4,16,66]{2,1,3,0:T(4,128)S(1)} %pad_maximum_fusion.2), channel_id=1, source_target_pairs={{0,4},{1,5},{2,6},{3,7},{4,0},{5,1},{6,2},{7,3},{8,12},{9,13},{10,... | collective-permute-start | bytes 101384 | tf_op jit(solution)/shard_map/ppermute | solution.py:66
  70.2 5.5 %collective-permute-done.2 = f32[2,4,16,66]{2,1,3,0:T(4,128)} collective-permute-done((f32[2,4,16,66]{2,1,3,0:T(4,128)S(1)}, f32[2,4,16,66]{2,1,3,0:T(4,128)}, u32[]{:S(2)}, u32[]{:S(2)}) %collective-permute-start.2) | collective-permute-done | bytes 33824 | tf_op jit(solution)/shard_map/ppermute | solution.py:66
  75.6 1.1 broadcast_select_fusion.5
  76.9 1.6 %collective-permute-start.3 = (f32[2,4,16,66]{2,1,3,0:T(4,128)S(1)}, f32[2,4,16,66]{2,1,3,0:T(4,128)S(1)}, u32[]{:S(2)}, u32[]{:S(2)}) collective-permute-start(f32[2,4,16,66]{2,1,3,0:T(4,128)S(1)} %pad_maximum_fusion.3), channel_id=1, source_target_pairs={{0,8},{1,9},{2,10},{3,11},{4,12},{5,13},{6,14},{7,15},{8,0},{9,1},... | collective-permute-start | bytes 101384 | tf_op jit(solution)/shard_map/ppermute | solution.py:66
  78.7 5.6 %collective-permute-done.3 = f32[2,4,16,66]{2,1,3,0:T(4,128)S(1)} collective-permute-done((f32[2,4,16,66]{2,1,3,0:T(4,128)S(1)}, f32[2,4,16,66]{2,1,3,0:T(4,128)S(1)}, u32[]{:S(2)}, u32[]{:S(2)}) %collective-permute-start.3) | collective-permute-done | bytes 33824 | tf_op jit(solution)/shard_map/ppermute | solution.py:66
  85.3 3.0 %collective-permute-start.4 = (f32[2,4,16,66]{2,1,3,0:T(4,128)}, f32[2,4,16,66]{2,1,3,0:T(4,128)}, u32[]{:S(2)}, u32[]{:S(2)}) collective-permute-start(f32[2,4,16,66]{2,1,3,0:T(4,128)} %pad_maximum_fusion.4), channel_id=1, source_target_pairs={{0,16},{1,17},{2,18},{3,19},{4,20},{5,21},{6,22},{7,23},{8,24},{9,... | collective-permute-start | bytes 101384 | tf_op jit(solution)/shard_map/ppermute | solution.py:66
  89.1 4.5 %collective-permute-done.4 = f32[2,4,16,66]{2,1,3,0:T(4,128)} collective-permute-done((f32[2,4,16,66]{2,1,3,0:T(4,128)}, f32[2,4,16,66]{2,1,3,0:T(4,128)}, u32[]{:S(2)}, u32[]{:S(2)}) %collective-permute-start.4) | collective-permute-done | bytes 33824 | tf_op jit(solution)/shard_map/ppermute | solution.py:66
  95.4 2.1 %fusion.149 = (f32[16]{0:T(128)S(1)}, f32[16,1024]{1,0:T(8,128)S(1)}) fusion(f32[16,1024]{1,0:T(8,128)S(1)} %reshape.258, bf16[16,1024]{1,0:T(8,128)(2,1)S(1)} %convert_element_type.78, bf16[1024,1024]{1,0:T(8,128)(2,1)} %all-gather.2.cloned.1.call-done), kind=kOutput, calls=%fused_computation.231 | convolution fusion | flops 33587184 | bytes 2261056 | tf_op jit(solution)/shard_map/dot_general | solution.py:141
  97.8 12.0 %all_gather.11 = bf16[64,1024]{1,0:T(8,128)(2,1)S(1)} all-gather(bf16[16,1024]{1,0:T(8,128)(2,1)S(1)} %multiply_convert_fusion), channel_id=1, replica_groups=mesh['req'=4,'seq'=32] {'req'}, dimensions={0}, use_global_device_ids=true | all-gather | bytes 163840 | tf_op jit(solution)/shard_map/all_gather | solution.py:145
  109.8 3.7 %fusion.38 = f32[64,1024]{1,0:T(8,128)} fusion(bf16[1024,1024]{1,0:T(8,128)(2,1)S(1)} %copy-done, bf16[64,1024]{1,0:T(8,128)(2,1)S(1)} %all_gather.11, bf16[1024,1024]{1,0:T(8,128)(2,1)} %param.30), kind=kOutput, calls=%fused_computation.77 | convolution fusion | flops 272695296 | bytes 4587520 | tf_op jit(solution)/shard_map/dot_general | solution.py:152
  116.1 18.5 %reduce-scatter.2.cloned.1.call-done = f32[16,1024]{1,0:T(8,128)} async-done(((f32[64,1024]{1,0:T(8,128)}), f32[16,1024]{1,0:T(8,128)}) %reduce-scatter.2.cloned.1.call-update) | async-done | bytes 65552 | tf_op jit(solution)/shard_map/reduce_scatter | solution.py:151
  (136 shorter events, 22.3 us)
Async XLA Ops:
  7.2 102.6 %copy-start = (bf16[1024,1024]{1,0:T(8,128)(2,1)S(1)}, bf16[1024,1024]{1,0:T(8,128)(2,1)}, u32[]{:S(2)}) copy-start(bf16[1024,1024]{1,0:T(8,128)(2,1)} %param.31) | copy-start | bytes 6291460
  24.1 7.8 %copy-start.16 = (s32[2]{0:T(128)S(1)}, s32[2]{0:T(128)}, u32[]{:S(2)}) copy-start(s32[2]{0:T(128)} %param.22) | copy-start | bytes 28
  24.1 7.9 %copy-start.17 = (s32[2]{0:T(128)S(1)}, s32[2]{0:T(128)}, u32[]{:S(2)}) copy-start(s32[2]{0:T(128)} %param.23) | copy-start | bytes 28
  26.5 10.1 %all-to-all-start = ((bf16[4,16,768]{2,1,0:T(8,128)(2,1)}), bf16[4,16,768]{2,1,0:T(8,128)(2,1)S(1)}, u32[]{:S(2)}, u32[]{:S(2)}) async-start(bf16[4,16,768]{2,1,0:T(8,128)(2,1)} %bitcast), calls=%async_computation | async-start | bytes 196608 | tf_op jit(solution)/shard_map/all_to_all | solution.py:125
  30.8 64.6 %all-gather.2.cloned.1.call-start = ((), (), s32[]{:S(2)}) async-start(), calls=%async_computation.2 | async-start | bytes 2621440 | tf_op jit(solution)/shard_map/all_gather | solution.py:109
  31.5 103.1 %reduce-scatter.2.cloned.1.call-start = ((), (), s32[]{:S(2)}) async-start(), calls=%async_computation.3 | async-start | bytes 327680 | tf_op jit(solution)/shard_map/reduce_scatter | solution.py:151
  44.2 4.1 %copy-start.1 = (bf16[2,1024,1024]{2,1,0:T(8,128)(2,1)S(1)}, bf16[2,1024,1024]{2,1,0:T(8,128)(2,1)}, u32[]{:S(2)}) copy-start(bf16[2,1024,1024]{2,1,0:T(8,128)(2,1)} %param.19) | copy-start | bytes 12582916
  50.5 2.7 %copy-start.3 = (bf16[16,4,1,256]{3,2,0,1:T(2,128)(2,1)S(1)}, bf16[16,4,1,256]{3,2,0,1:T(2,128)(2,1)}, u32[]{:S(2)}) copy-start(bf16[16,4,1,256]{3,2,0,1:T(2,128)(2,1)} %get-tuple-element.46) | copy-start | bytes 98308
  52.6 5.6 %copy-start.15 = (pred[4,4]{1,0:T(4,128)(4,1)S(1)}, pred[4,4]{1,0:T(4,128)(4,1)}, u32[]{:S(2)}) copy-start(pred[4,4]{1,0:T(4,128)(4,1)} %iota_compare_fusion.2) | copy-start | bytes 52
  53.0 2.2 %collective-permute-start = (f32[2,4,16,66]{2,1,3,0:T(4,128)S(1)}, f32[2,4,16,66]{2,1,3,0:T(4,128)}, u32[]{:S(2)}, u32[]{:S(2)}) collective-permute-start(f32[2,4,16,66]{2,1,3,0:T(4,128)S(1)} %pad_maximum_fusion), channel_id=1, source_target_pairs={{0,1},{1,0},{2,3},{3,2},{4,5},{5,4},{6,7},{7,6},{8,9},{9,8},{10,11... | collective-permute-start | bytes 101384 | tf_op jit(solution)/shard_map/ppermute | solution.py:66
  56.3 13.7 %copy-start.2 = (bf16[16,4,1,256]{3,2,0,1:T(2,128)(2,1)S(1)}, bf16[16,4,1,256]{3,2,0,1:T(2,128)(2,1)}, u32[]{:S(2)}) copy-start(bf16[16,4,1,256]{3,2,0,1:T(2,128)(2,1)} %get-tuple-element.45) | copy-start | bytes 98308
  56.5 8.9 %collective-permute-start.1 = (f32[2,4,16,66]{2,1,3,0:T(4,128)S(1)}, f32[2,4,16,66]{2,1,3,0:T(4,128)S(1)}, u32[]{:S(2)}, u32[]{:S(2)}) collective-permute-start(f32[2,4,16,66]{2,1,3,0:T(4,128)S(1)} %pad_maximum_fusion.1), channel_id=1, source_target_pairs={{0,2},{1,3},{2,0},{3,1},{4,6},{5,7},{6,4},{7,5},{8,10},{9,11},{10,... | collective-permute-start | bytes 101384 | tf_op jit(solution)/shard_map/ppermute | solution.py:66
  58.3 11.5 %copy-start.9 = (f32[4,4,16]{2,1,0:T(4,128)}, f32[4,4,16]{2,1,0:T(4,128)S(1)}, u32[]{:S(2)}) copy-start(f32[4,4,16]{2,1,0:T(4,128)S(1)} %fusion.84) | copy-start | bytes 3076
  65.8 9.8 %collective-permute-start.2 = (f32[2,4,16,66]{2,1,3,0:T(4,128)S(1)}, f32[2,4,16,66]{2,1,3,0:T(4,128)}, u32[]{:S(2)}, u32[]{:S(2)}) collective-permute-start(f32[2,4,16,66]{2,1,3,0:T(4,128)S(1)} %pad_maximum_fusion.2), channel_id=1, source_target_pairs={{0,4},{1,5},{2,6},{3,7},{4,0},{5,1},{6,2},{7,3},{8,12},{9,13},{10,... | collective-permute-start | bytes 101384 | tf_op jit(solution)/shard_map/ppermute | solution.py:66
  76.7 11.6 %copy-start.13 = (f32[2,64]{1,0:T(2,128)S(1)}, f32[2,64]{1,0:T(2,128)}, u32[]{:S(2)}) copy-start(f32[2,64]{1,0:T(2,128)} %copy-done.12) | copy-start | bytes 1540
  76.9 7.3 %collective-permute-start.3 = (f32[2,4,16,66]{2,1,3,0:T(4,128)S(1)}, f32[2,4,16,66]{2,1,3,0:T(4,128)S(1)}, u32[]{:S(2)}, u32[]{:S(2)}) collective-permute-start(f32[2,4,16,66]{2,1,3,0:T(4,128)S(1)} %pad_maximum_fusion.3), channel_id=1, source_target_pairs={{0,8},{1,9},{2,10},{3,11},{4,12},{5,13},{6,14},{7,15},{8,0},{9,1},... | collective-permute-start | bytes 101384 | tf_op jit(solution)/shard_map/ppermute | solution.py:66
  84.4 10.3 %copy-start.10 = (f32[4,4,16]{2,1,0:T(4,128)S(1)}, f32[4,4,16]{2,1,0:T(4,128)}, u32[]{:S(2)}) copy-start(f32[4,4,16]{2,1,0:T(4,128)} %copy-done.9) | copy-start | bytes 3076
  84.4 10.3 %copy-start.11 = (f32[4,4,16]{2,1,0:T(4,128)S(1)}, f32[4,4,16]{2,1,0:T(4,128)}, u32[]{:S(2)}) copy-start(f32[4,4,16]{2,1,0:T(4,128)} %get-tuple-element.48) | copy-start | bytes 3076
  85.3 8.3 %collective-permute-start.4 = (f32[2,4,16,66]{2,1,3,0:T(4,128)}, f32[2,4,16,66]{2,1,3,0:T(4,128)}, u32[]{:S(2)}, u32[]{:S(2)}) collective-permute-start(f32[2,4,16,66]{2,1,3,0:T(4,128)} %pad_maximum_fusion.4), channel_id=1, source_target_pairs={{0,16},{1,17},{2,18},{3,19},{4,20},{5,21},{6,22},{7,23},{8,24},{9,... | collective-permute-start | bytes 101384 | tf_op jit(solution)/shard_map/ppermute | solution.py:66
  94.8 2.9 %copy-start.14 = (f32[1024]{0:T(1024)S(1)}, f32[1024]{0:T(1024)}, u32[]{:S(2)}) copy-start(f32[1024]{0:T(1024)} %param.25) | copy-start | bytes 12292
  109.8 3.8 %copy-start.8 = (bf16[8,4,1,256]{3,2,0,1:T(2,128)(2,1)S(1)}, bf16[8,4,1,256]{3,2,0,1:T(2,128)(2,1)}, u32[]{:S(2)}) copy-start(bf16[8,4,1,256]{3,2,0,1:T(2,128)(2,1)} %get-tuple-element.42) | copy-start | bytes 49156
  109.8 4.4 %copy-start.7 = (bf16[8,4,1,256]{3,2,0,1:T(2,128)(2,1)S(1)}, bf16[8,4,1,256]{3,2,0,1:T(2,128)(2,1)}, u32[]{:S(2)}) copy-start(bf16[8,4,1,256]{3,2,0,1:T(2,128)(2,1)} %get-tuple-element.41) | copy-start | bytes 49156
  109.8 5.0 %copy-start.6 = (bf16[8,4,1,256]{3,2,0,1:T(2,128)(2,1)S(1)}, bf16[8,4,1,256]{3,2,0,1:T(2,128)(2,1)}, u32[]{:S(2)}) copy-start(bf16[8,4,1,256]{3,2,0,1:T(2,128)(2,1)} %get-tuple-element.40) | copy-start | bytes 49156
  109.8 5.7 %copy-start.5 = (bf16[8,4,1,256]{3,2,0,1:T(2,128)(2,1)S(1)}, bf16[8,4,1,256]{3,2,0,1:T(2,128)(2,1)}, u32[]{:S(2)}) copy-start(bf16[8,4,1,256]{3,2,0,1:T(2,128)(2,1)} %get-tuple-element.39) | copy-start | bytes 49156
  (2 other events, 3.5 us)
Sparse Core Ops, SparseCore 0:
  33.3 32.8 all-gather.1
  113.7 20.9 reduce-scatter.1
where the time goes:
time: 144 us
  waiting for transfers between devices  45.9 us (32%)
  blocking collectives  25.3 us (18%)
  matrix products  17.7 us (12%)
  between operations  14.6 us (10%)
  other arithmetic  13.9 us (10%)
  starting transfers between devices  13.9 us (10%)
  local copies, waits for them, and re-layouts  12.2 us (8%)
    ppermute x5, waiting for transfers between devices, merge_long(): other = lax.ppermute(packed, 'seq', pairs)  22.6 us
    reduce_scatter x1, waiting for transfers between devices, shards(): lax.psum_scatter(jnp.dot(hidden, w_down, preferred_element_type=jnp.float...  18.5 us
    all_gather x1, blocking collectives, shards(): lax.all_gather(normed, 'req', axis=0, tiled=True)  13.3 us
    all_gather x1, blocking collectives, shards(): lax.all_gather(normed_ffn, 'req', axis=0, tiled=True)  12 us
    ppermute x5, starting transfers between devices, merge_long(): other = lax.ppermute(packed, 'seq', pairs)  9.6 us
    dot_general x2, matrix products, cache_block(): jnp.einsum('rnc,rpc->rnp', spread, keys, preferred_element_type=jnp.float32)  5.82 us
    all_to_all x1, starting transfers between devices, shards(): lax.all_to_all(project_spread, 'req', split_axis=0, concat_axis=1, tiled=...  4.26 us
    all_to_all x1, waiting for transfers between devices, shards(): lax.all_to_all(project_spread, 'req', split_axis=0, concat_axis=1, tiled=...  4 us
  transfers between devices with their start and end apart: 8, of which 6 were waited for; matrix products, arithmetic and copies ran while one was open for 21% of the time, Pallas kernels for 0%

commit v1 on v0

--- a/solution.py
+++ b/solution.py
@@ -122,7 +122,12 @@
         stacked,
         preferred_element_type=jnp.float32,
     ).astype(jnp.bfloat16)
-    moved = lax.all_to_all(project_spread, "req", split_axis=0, concat_axis=1, tiled=True)
+    moved = jnp.concatenate(
+        lax.all_to_all(
+            jnp.stack(jnp.split(project_spread, lax.axis_size("req"), axis=0)), "req", 0, 0
+        ),
+        axis=1,
+    )
     moved = moved.reshape(rows_count, groups, 3, local)
     query = moved[:, :, 0].reshape(req_count, steps, H, HD)
     key_now = moved[:, :, 1].reshape(req_count, steps, width)

time: 144 us -> 144 us (level)
  no operation moved by 1% of the time
where the time goes in v1:
time: 144 us
  waiting for transfers between devices  45.9 us (32%)
  blocking collectives  25.3 us (18%)
  matrix products  17.1 us (12%)
  other arithmetic  14.6 us (10%)
  between operations  14.6 us (10%)
  starting transfers between devices  13.9 us (10%)
  local copies, waits for them, and re-layouts  12.2 us (8%)
    ppermute x5, waiting for transfers between devices, merge_long(): other = lax.ppermute(packed, 'seq', pairs)  22.6 us
    reduce_scatter x1, waiting for transfers between devices, shards(): lax.psum_scatter(jnp.dot(hidden, w_down, preferred_element_type=jnp.float...  18.5 us
    all_gather x1, blocking collectives, shards(): lax.all_gather(normed, 'req', axis=0, tiled=True)  13.3 us
    all_gather x1, blocking collectives, shards(): lax.all_gather(normed_ffn, 'req', axis=0, tiled=True)  12 us
    ppermute x5, starting transfers between devices, merge_long(): other = lax.ppermute(packed, 'seq', pairs)  9.62 us
    dot_general x2, matrix products, cache_block(): jnp.einsum('rnc,rpc->rnp', spread, keys, preferred_element_type=jnp.float32)  5.82 us
    all_to_all x1, starting transfers between devices, shards(): lax.all_to_all(jnp.stack(jnp.split(project_spread, lax.axis_size('req'),...  4.26 us
    all_to_all x1, waiting for transfers between devices, shards(): lax.all_to_all(jnp.stack(jnp.split(project_spread, lax.axis_size('req'),...  4 us
  transfers between devices with their start and end apart: 8, of which 6 were waited for; matrix products, arithmetic and copies ran while one was open for 21% of the time, Pallas kernels for 0%

profile of v1, /device:TPU:0, one launch (start us, length us, event | category | flops | bytes accessed | tf_op | source)
XLA Modules:
  0.0 143.6 jit_solution(9744866087891835197)
XLA Ops:
  10.8 13.3 %all_gather.9 = bf16[64,1024]{1,0:T(8,128)(2,1)S(1)} all-gather(bf16[16,1024]{1,0:T(8,128)(2,1)S(1)} %multiply_convert_fusion.1), channel_id=1, replica_groups=mesh['req'=4,'seq'=32] {'req'}, dimensions={0}, use_global_device_ids=true | all-gather | bytes 163840 | tf_op jit(solution)/shard_map/all_gather | solution.py:121
  24.1 1.8 %fusion.7 = bf16[64,768]{1,0:T(8,128)(2,1)S(1)} fusion(bf16[64,1024]{1,0:T(8,128)(2,1)S(1)} %all_gather.9, bf16[1024,256]{1,0:T(8,128)(2,1)} %param.28, bf16[1024,256]{1,0:T(8,128)(2,1)} %param.27, bf16[1024,256]{1,0:T(8,128)(2,1)} %param.26), kind=kOutput, calls=%fused_computation.8 | convolution fusion | flops 105431040 | bytes 1802240 | tf_op jit(solution)/shard_map/dot_general | solution.py:120
  26.6 4.3 %all-to-all-start = ((bf16[4,16,768]{2,1,0:T(8,128)(2,1)}), bf16[4,16,768]{2,1,0:T(8,128)(2,1)S(1)}, u32[]{:S(2)}, u32[]{:S(2)}) async-start(bf16[4,16,768]{2,1,0:T(8,128)(2,1)} %pad_maximum_fusion.5), calls=%async_computation | async-start | bytes 196608 | tf_op jit(solution)/shard_map/all_to_all | solution.py:126
  32.6 4.0 %all-to-all-done = bf16[4,16,768]{2,1,0:T(8,128)(2,1)S(1)} async-done(((bf16[4,16,768]{2,1,0:T(8,128)(2,1)}), bf16[4,16,768]{2,1,0:T(8,128)(2,1)S(1)}, u32[]{:S(2)}, u32[]{:S(2)}) %all-to-all-start) | async-done | bytes 98336 | tf_op jit(solution)/shard_map/all_to_all | solution.py:126
  38.8 1.8 %fusion.147 = (f32[2,64]{1,0:T(2,128)S(1)}, f32[2,64,256]{2,1,0:T(8,128)S(1)}) fusion(bf16[2,256,1024]{2,1,0:T(8,128)(2,1)} %param.20, bf16[2,64,1024]{2,1,0:T(8,128)(2,1)S(1)} %mul.317, bf16[64,1024]{1,0:T(8,128)(2,1)S(1)} %mul.307, pred[2,256]{1,0:T(4,128)(4,1)S(1)} %broadcast_compare_fusion), kind=kOutput, calls=%fused_computation.234 | convolution fusion | flops 67338112 | bytes 1573888 | tf_op jit(solution)/shard_map/rnc,rpc->rnp/dot_general | solution.py:36
  40.9 1.6 %fusion.74 = f32[2,64,1024]{2,1,0:T(8,128)S(1)} fusion(bf16[2,256,1024]{2,1,0:T(8,128)(2,1)} %param.21, f32[2,64,256]{2,1,0:T(8,128)S(1)} %get-tuple-element.59, f32[2,64]{1,0:T(2,128)S(1)} %get-tuple-element.58, pred[2,256]{1,0:T(4,128)(4,1)S(1)} %broadcast_compare_fusion), kind=kOutput, calls=%fused_computation.114 | convolution fusion | flops 67207168 | bytes 1704960 | tf_op jit(solution)/shard_map/rnp,rpc->rnc/dot_general | solution.py:41
  42.4 1.3 reshape.253
  44.3 4.1 %fusion.148 = (f32[2,64]{1,0:T(2,128)S(1)}, f32[2,64,1024]{2,1,0:T(8,128)S(1)}) fusion(bf16[2,1024,1024]{2,1,0:T(8,128)(2,1)} %param.18, bf16[2,64,1024]{2,1,0:T(8,128)(2,1)S(1)} %mul.305, bf16[64,1024]{1,0:T(8,128)(2,1)S(1)} %mul.307, pred[2,1024]{1,0:T(4,128)(4,1)S(1)} %iota_compare_fusion.1), kind=kOutput, calls=%fused_computation.235 | convolution fusion | flops 268959616 | bytes 5114368 | tf_op jit(solution)/shard_map/rnc,rpc->rnp/dot_general | solution.py:36
  49.3 1.2 reshape.252
  50.5 2.1 %multiply_reduce_fusion.1 = (f32[2,4,16,64]{3,2,1,0:T(8,128)S(1)}, f32[2,4,16,64]{3,2,1,0:T(8,128)S(1)}) fusion(f32[2,4,16,16,64]{4,3,2,1,0:T(8,128)} %reshape.252, f32[16,16]{1,0:T(8,128)S(1)} %fusion.97, f32[2,4,16,16,64]{4,3,2,1,0:T(8,128)} %reshape.253), kind=kLoop, calls=%fused_computation.13 | loop fusion | flops 507904 | bytes 1115136 | tf_op jit(solution)/shard_map/reduce_sum | solution.py:44
  55.3 1.1 broadcast_select_fusion.1
  56.6 1.7 %collective-permute-start.1 = (f32[2,4,16,66]{2,1,3,0:T(4,128)S(1)}, f32[2,4,16,66]{2,1,3,0:T(4,128)S(1)}, u32[]{:S(2)}, u32[]{:S(2)}) collective-permute-start(f32[2,4,16,66]{2,1,3,0:T(4,128)S(1)} %pad_maximum_fusion.1), channel_id=1, source_target_pairs={{0,2},{1,3},{2,0},{3,1},{4,6},{5,7},{6,4},{7,5},{8,10},{9,11},{10,... | collective-permute-start | bytes 101384 | tf_op jit(solution)/shard_map/ppermute | solution.py:66
  58.3 7.2 %collective-permute-done.1 = f32[2,4,16,66]{2,1,3,0:T(4,128)S(1)} collective-permute-done((f32[2,4,16,66]{2,1,3,0:T(4,128)S(1)}, f32[2,4,16,66]{2,1,3,0:T(4,128)S(1)}, u32[]{:S(2)}, u32[]{:S(2)}) %collective-permute-start.1) | collective-permute-done | bytes 33824 | tf_op jit(solution)/shard_map/ppermute | solution.py:66
  65.8 3.3 %collective-permute-start.2 = (f32[2,4,16,66]{2,1,3,0:T(4,128)S(1)}, f32[2,4,16,66]{2,1,3,0:T(4,128)}, u32[]{:S(2)}, u32[]{:S(2)}) collective-permute-start(f32[2,4,16,66]{2,1,3,0:T(4,128)S(1)} %pad_maximum_fusion.2), channel_id=1, source_target_pairs={{0,4},{1,5},{2,6},{3,7},{4,0},{5,1},{6,2},{7,3},{8,12},{9,13},{10,... | collective-permute-start | bytes 101384 | tf_op jit(solution)/shard_map/ppermute | solution.py:66
  70.2 5.4 %collective-permute-done.2 = f32[2,4,16,66]{2,1,3,0:T(4,128)} collective-permute-done((f32[2,4,16,66]{2,1,3,0:T(4,128)S(1)}, f32[2,4,16,66]{2,1,3,0:T(4,128)}, u32[]{:S(2)}, u32[]{:S(2)}) %collective-permute-start.2) | collective-permute-done | bytes 33824 | tf_op jit(solution)/shard_map/ppermute | solution.py:66
  75.6 1.1 broadcast_select_fusion.5
  76.9 1.6 %collective-permute-start.3 = (f32[2,4,16,66]{2,1,3,0:T(4,128)S(1)}, f32[2,4,16,66]{2,1,3,0:T(4,128)S(1)}, u32[]{:S(2)}, u32[]{:S(2)}) collective-permute-start(f32[2,4,16,66]{2,1,3,0:T(4,128)S(1)} %pad_maximum_fusion.3), channel_id=1, source_target_pairs={{0,8},{1,9},{2,10},{3,11},{4,12},{5,13},{6,14},{7,15},{8,0},{9,1},... | collective-permute-start | bytes 101384 | tf_op jit(solution)/shard_map/ppermute | solution.py:66
  78.7 5.6 %collective-permute-done.3 = f32[2,4,16,66]{2,1,3,0:T(4,128)S(1)} collective-permute-done((f32[2,4,16,66]{2,1,3,0:T(4,128)S(1)}, f32[2,4,16,66]{2,1,3,0:T(4,128)S(1)}, u32[]{:S(2)}, u32[]{:S(2)}) %collective-permute-start.3) | collective-permute-done | bytes 33824 | tf_op jit(solution)/shard_map/ppermute | solution.py:66
  85.3 3.0 %collective-permute-start.4 = (f32[2,4,16,66]{2,1,3,0:T(4,128)}, f32[2,4,16,66]{2,1,3,0:T(4,128)}, u32[]{:S(2)}, u32[]{:S(2)}) collective-permute-start(f32[2,4,16,66]{2,1,3,0:T(4,128)} %pad_maximum_fusion.4), channel_id=1, source_target_pairs={{0,16},{1,17},{2,18},{3,19},{4,20},{5,21},{6,22},{7,23},{8,24},{9,... | collective-permute-start | bytes 101384 | tf_op jit(solution)/shard_map/ppermute | solution.py:66
  89.1 4.4 %collective-permute-done.4 = f32[2,4,16,66]{2,1,3,0:T(4,128)} collective-permute-done((f32[2,4,16,66]{2,1,3,0:T(4,128)}, f32[2,4,16,66]{2,1,3,0:T(4,128)}, u32[]{:S(2)}, u32[]{:S(2)}) %collective-permute-start.4) | collective-permute-done | bytes 33824 | tf_op jit(solution)/shard_map/ppermute | solution.py:66
  95.4 2.1 %fusion.149 = (f32[16]{0:T(128)S(1)}, f32[16,1024]{1,0:T(8,128)S(1)}) fusion(f32[16,1024]{1,0:T(8,128)S(1)} %reshape.254, bf16[16,1024]{1,0:T(8,128)(2,1)S(1)} %convert_element_type.78, bf16[1024,1024]{1,0:T(8,128)(2,1)} %all-gather.2.cloned.1.call-done), kind=kOutput, calls=%fused_computation.236 | convolution fusion | flops 33587184 | bytes 2261056 | tf_op jit(solution)/shard_map/dot_general | solution.py:146
  97.8 12.0 %all_gather.11 = bf16[64,1024]{1,0:T(8,128)(2,1)S(1)} all-gather(bf16[16,1024]{1,0:T(8,128)(2,1)S(1)} %multiply_convert_fusion), channel_id=1, replica_groups=mesh['req'=4,'seq'=32] {'req'}, dimensions={0}, use_global_device_ids=true | all-gather | bytes 163840 | tf_op jit(solution)/shard_map/all_gather | solution.py:150
  109.8 3.7 %fusion.38 = f32[64,1024]{1,0:T(8,128)} fusion(bf16[1024,1024]{1,0:T(8,128)(2,1)S(1)} %copy-done, bf16[64,1024]{1,0:T(8,128)(2,1)S(1)} %all_gather.11, bf16[1024,1024]{1,0:T(8,128)(2,1)} %param.30), kind=kOutput, calls=%fused_computation.77 | convolution fusion | flops 272695296 | bytes 4587520 | tf_op jit(solution)/shard_map/dot_general | solution.py:157
  116.1 18.5 %reduce-scatter.2.cloned.1.call-done = f32[16,1024]{1,0:T(8,128)} async-done(((f32[64,1024]{1,0:T(8,128)}), f32[16,1024]{1,0:T(8,128)}) %reduce-scatter.2.cloned.1.call-update) | async-done | bytes 65552 | tf_op jit(solution)/shard_map/reduce_scatter | solution.py:156
  (138 shorter events, 22.9 us)
Async XLA Ops:
  7.2 102.6 %copy-start = (bf16[1024,1024]{1,0:T(8,128)(2,1)S(1)}, bf16[1024,1024]{1,0:T(8,128)(2,1)}, u32[]{:S(2)}) copy-start(bf16[1024,1024]{1,0:T(8,128)(2,1)} %param.31) | copy-start | bytes 6291460
  24.1 7.8 %copy-start.16 = (s32[2]{0:T(128)S(1)}, s32[2]{0:T(128)}, u32[]{:S(2)}) copy-start(s32[2]{0:T(128)} %param.22) | copy-start | bytes 28
  24.1 7.9 %copy-start.17 = (s32[2]{0:T(128)S(1)}, s32[2]{0:T(128)}, u32[]{:S(2)}) copy-start(s32[2]{0:T(128)} %param.23) | copy-start | bytes 28
  26.6 10.1 %all-to-all-start = ((bf16[4,16,768]{2,1,0:T(8,128)(2,1)}), bf16[4,16,768]{2,1,0:T(8,128)(2,1)S(1)}, u32[]{:S(2)}, u32[]{:S(2)}) async-start(bf16[4,16,768]{2,1,0:T(8,128)(2,1)} %pad_maximum_fusion.5), calls=%async_computation | async-start | bytes 196608 | tf_op jit(solution)/shard_map/all_to_all | solution.py:126
  30.8 64.6 %all-gather.2.cloned.1.call-start = ((), (), s32[]{:S(2)}) async-start(), calls=%async_computation.2 | async-start | bytes 2621440 | tf_op jit(solution)/shard_map/all_gather | solution.py:109
  31.6 103.1 %reduce-scatter.2.cloned.1.call-start = ((), (), s32[]{:S(2)}) async-start(), calls=%async_computation.3 | async-start | bytes 327680 | tf_op jit(solution)/shard_map/reduce_scatter | solution.py:156
  44.3 4.1 %copy-start.1 = (bf16[2,1024,1024]{2,1,0:T(8,128)(2,1)S(1)}, bf16[2,1024,1024]{2,1,0:T(8,128)(2,1)}, u32[]{:S(2)}) copy-start(bf16[2,1024,1024]{2,1,0:T(8,128)(2,1)} %param.19) | copy-start | bytes 12582916
  50.5 2.7 %copy-start.3 = (bf16[16,4,1,256]{3,2,0,1:T(2,128)(2,1)S(1)}, bf16[16,4,1,256]{3,2,0,1:T(2,128)(2,1)}, u32[]{:S(2)}) copy-start(bf16[16,4,1,256]{3,2,0,1:T(2,128)(2,1)} %get-tuple-element.46) | copy-start | bytes 98308
  52.7 5.6 %copy-start.15 = (pred[4,4]{1,0:T(4,128)(4,1)S(1)}, pred[4,4]{1,0:T(4,128)(4,1)}, u32[]{:S(2)}) copy-start(pred[4,4]{1,0:T(4,128)(4,1)} %iota_compare_fusion.2) | copy-start | bytes 52
  53.0 2.3 %collective-permute-start = (f32[2,4,16,66]{2,1,3,0:T(4,128)S(1)}, f32[2,4,16,66]{2,1,3,0:T(4,128)}, u32[]{:S(2)}, u32[]{:S(2)}) collective-permute-start(f32[2,4,16,66]{2,1,3,0:T(4,128)S(1)} %pad_maximum_fusion), channel_id=1, source_target_pairs={{0,1},{1,0},{2,3},{3,2},{4,5},{5,4},{6,7},{7,6},{8,9},{9,8},{10,11... | collective-permute-start | bytes 101384 | tf_op jit(solution)/shard_map/ppermute | solution.py:66
  56.4 13.7 %copy-start.2 = (bf16[16,4,1,256]{3,2,0,1:T(2,128)(2,1)S(1)}, bf16[16,4,1,256]{3,2,0,1:T(2,128)(2,1)}, u32[]{:S(2)}) copy-start(bf16[16,4,1,256]{3,2,0,1:T(2,128)(2,1)} %get-tuple-element.45) | copy-start | bytes 98308
  56.6 8.9 %collective-permute-start.1 = (f32[2,4,16,66]{2,1,3,0:T(4,128)S(1)}, f32[2,4,16,66]{2,1,3,0:T(4,128)S(1)}, u32[]{:S(2)}, u32[]{:S(2)}) collective-permute-start(f32[2,4,16,66]{2,1,3,0:T(4,128)S(1)} %pad_maximum_fusion.1), channel_id=1, source_target_pairs={{0,2},{1,3},{2,0},{3,1},{4,6},{5,7},{6,4},{7,5},{8,10},{9,11},{10,... | collective-permute-start | bytes 101384 | tf_op jit(solution)/shard_map/ppermute | solution.py:66
  58.3 11.5 %copy-start.9 = (f32[4,4,16]{2,1,0:T(4,128)}, f32[4,4,16]{2,1,0:T(4,128)S(1)}, u32[]{:S(2)}) copy-start(f32[4,4,16]{2,1,0:T(4,128)S(1)} %fusion.84) | copy-start | bytes 3076
  65.8 9.8 %collective-permute-start.2 = (f32[2,4,16,66]{2,1,3,0:T(4,128)S(1)}, f32[2,4,16,66]{2,1,3,0:T(4,128)}, u32[]{:S(2)}, u32[]{:S(2)}) collective-permute-start(f32[2,4,16,66]{2,1,3,0:T(4,128)S(1)} %pad_maximum_fusion.2), channel_id=1, source_target_pairs={{0,4},{1,5},{2,6},{3,7},{4,0},{5,1},{6,2},{7,3},{8,12},{9,13},{10,... | collective-permute-start | bytes 101384 | tf_op jit(solution)/shard_map/ppermute | solution.py:66
  76.7 11.6 %copy-start.13 = (f32[2,64]{1,0:T(2,128)S(1)}, f32[2,64]{1,0:T(2,128)}, u32[]{:S(2)}) copy-start(f32[2,64]{1,0:T(2,128)} %copy-done.12) | copy-start | bytes 1540
  76.9 7.3 %collective-permute-start.3 = (f32[2,4,16,66]{2,1,3,0:T(4,128)S(1)}, f32[2,4,16,66]{2,1,3,0:T(4,128)S(1)}, u32[]{:S(2)}, u32[]{:S(2)}) collective-permute-start(f32[2,4,16,66]{2,1,3,0:T(4,128)S(1)} %pad_maximum_fusion.3), channel_id=1, source_target_pairs={{0,8},{1,9},{2,10},{3,11},{4,12},{5,13},{6,14},{7,15},{8,0},{9,1},... | collective-permute-start | bytes 101384 | tf_op jit(solution)/shard_map/ppermute | solution.py:66
  84.4 10.3 %copy-start.10 = (f32[4,4,16]{2,1,0:T(4,128)S(1)}, f32[4,4,16]{2,1,0:T(4,128)}, u32[]{:S(2)}) copy-start(f32[4,4,16]{2,1,0:T(4,128)} %copy-done.9) | copy-start | bytes 3076
  84.4 10.3 %copy-start.11 = (f32[4,4,16]{2,1,0:T(4,128)S(1)}, f32[4,4,16]{2,1,0:T(4,128)}, u32[]{:S(2)}) copy-start(f32[4,4,16]{2,1,0:T(4,128)} %get-tuple-element.52) | copy-start | bytes 3076
  85.3 8.3 %collective-permute-start.4 = (f32[2,4,16,66]{2,1,3,0:T(4,128)}, f32[2,4,16,66]{2,1,3,0:T(4,128)}, u32[]{:S(2)}, u32[]{:S(2)}) collective-permute-start(f32[2,4,16,66]{2,1,3,0:T(4,128)} %pad_maximum_fusion.4), channel_id=1, source_target_pairs={{0,16},{1,17},{2,18},{3,19},{4,20},{5,21},{6,22},{7,23},{8,24},{9,... | collective-permute-start | bytes 101384 | tf_op jit(solution)/shard_map/ppermute | solution.py:66
  94.8 2.9 %copy-start.14 = (f32[1024]{0:T(1024)S(1)}, f32[1024]{0:T(1024)}, u32[]{:S(2)}) copy-start(f32[1024]{0:T(1024)} %param.25) | copy-start | bytes 12292
  109.8 3.8 %copy-start.8 = (bf16[8,4,1,256]{3,2,0,1:T(2,128)(2,1)S(1)}, bf16[8,4,1,256]{3,2,0,1:T(2,128)(2,1)}, u32[]{:S(2)}) copy-start(bf16[8,4,1,256]{3,2,0,1:T(2,128)(2,1)} %get-tuple-element.42) | copy-start | bytes 49156
  109.8 4.4 %copy-start.7 = (bf16[8,4,1,256]{3,2,0,1:T(2,128)(2,1)S(1)}, bf16[8,4,1,256]{3,2,0,1:T(2,128)(2,1)}, u32[]{:S(2)}) copy-start(bf16[8,4,1,256]{3,2,0,1:T(2,128)(2,1)} %get-tuple-element.41) | copy-start | bytes 49156
  109.8 5.0 %copy-start.6 = (bf16[8,4,1,256]{3,2,0,1:T(2,128)(2,1)S(1)}, bf16[8,4,1,256]{3,2,0,1:T(2,128)(2,1)}, u32[]{:S(2)}) copy-start(bf16[8,4,1,256]{3,2,0,1:T(2,128)(2,1)} %get-tuple-element.40) | copy-start | bytes 49156
  109.8 5.7 %copy-start.5 = (bf16[8,4,1,256]{3,2,0,1:T(2,128)(2,1)S(1)}, bf16[8,4,1,256]{3,2,0,1:T(2,128)(2,1)}, u32[]{:S(2)}) copy-start(bf16[8,4,1,256]{3,2,0,1:T(2,128)(2,1)} %get-tuple-element.39) | copy-start | bytes 49156
  (2 other events, 3.5 us)
Sparse Core Ops, SparseCore 0:
  33.3 32.8 all-gather.1
  113.7 20.9 reduce-scatter.1
